TPU v7x, 512 devices: a whole 4x8x8 slice. The times are simulated.
512 devices in a mesh: dp: 2 (over core), section: 8 (over z), mem: 32 (over y, x).
Axes of the slice: x: 4, y: 8, z: 8, core: 2. Of those that a mesh axis runs over, the one named last changes fastest.
Arguments:
- qkv_rows: bfloat16 [8, 64, 128, 3072], P('section', ('dp', 'mem')), may hold values from -5 to 5
- grad_output: bfloat16 [8, 64, 128, 2048], P('section', ('dp', 'mem')), may hold values from -12 to 12
- memory_rows: bfloat16 [8, 256, 64, 1024], P('section', 'mem'), may hold values from -5 to 5
- shard_fill: int32 [8, 32], P('section', 'mem'), may hold values from 257 to 512, as said below
- block_ids: int32 [8, 64, 2, 8], P('section', ('dp', 'mem')), may hold values from 0 to 255, as said below
Outputs:
- upstream: bfloat16 [8, 64, 128, 3072], P('section', ('dp', 'mem'))
- memory_grad: bfloat16 [8, 256, 64, 1024], P('section', 'mem')
Inputs may be any that keep to these rules, and one draw needn't show every extreme that they name: `shard_fill`: memory tokens at or beyond a shard's fill are empty. In every section one shard is full and one holds 257 tokens. `block_ids`: each query block names 8 blocks of different shards; all query blocks of one sequence together name at most one distinct block of any one shard; every named block holds a live token.
All inputs are finite; a program needn't handle non-finite values.
Results may differ from a plain program's by a relative error of at most 0.011.
Values may be sent and summed in bfloat16 or wider, within the bound.
No kernel may reach another device: no remote copies, remote signals or barrier semaphores. Data moves between devices by JAX's collectives and lax.ppermute only.
A program may use at most 128 MiB of HBM per device.

v0:
```python
from functools import partial
import jax
import jax.numpy as jnp
from jax import lax
from jax.sharding import PartitionSpec as P

H = 16
KEY_VALUE_HEADS = 4
DH = 128
BLK = 64
NEG_FILL = -1e30


def passed_along(array, axis, by):
    devices = lax.axis_size(axis)
    pairs = [(i, i + by) for i in range(devices) if 0 <= i + by < devices]
    return lax.ppermute(array, axis, pairs)


def head_scores(key_mask, queries, key_rows):
    raw = jnp.einsum(
        "bihd,bnd->bihn", queries, key_rows, preferred_element_type=jnp.float32
    ) * DH ** (-0.5)
    return jnp.where(key_mask[:, :, None, :], raw, NEG_FILL)


def head_forward(key_mask, pieces):
    queries, key_rows, value_rows = pieces
    scores = head_scores(key_mask, queries, key_rows)
    row_max = jnp.max(scores, axis=-1, keepdims=True)
    log_total = row_max + jnp.log(jnp.sum(jnp.exp(scores - row_max), axis=-1, keepdims=True))
    prob_bf = jnp.exp(scores - log_total).astype(jnp.bfloat16)
    attended = jnp.einsum(
        "bihn,bnd->bihd", prob_bf, value_rows, preferred_element_type=jnp.float32
    ).astype(jnp.bfloat16)
    return (log_total, attended)


def head_backward(key_mask, pieces):
    queries, key_rows, value_rows, grad_rows, log_total, attended = pieces
    scores = head_scores(key_mask, queries, key_rows)
    weights = jnp.exp(scores - log_total)
    prob_bf = weights.astype(jnp.bfloat16)
    dprobs = jnp.einsum("bihd,bnd->bihn", grad_rows, value_rows, preferred_element_type=jnp.float32)
    row_delta = jnp.sum(
        grad_rows.astype(jnp.float32) * attended.astype(jnp.float32), axis=-1, keepdims=True
    )
    dscores = (weights * (dprobs - row_delta)).astype(jnp.bfloat16)
    inv_root = DH ** (-0.5)
    grad_query = (
        jnp.einsum("bihn,bnd->bihd", dscores, key_rows, preferred_element_type=jnp.float32)
        * inv_root
    )
    grad_key = (
        jnp.einsum("bihn,bihd->bnd", dscores, queries, preferred_element_type=jnp.float32)
        * inv_root
    )
    grad_value = jnp.einsum(
        "bihn,bihd->bnd", prob_bf, grad_rows, preferred_element_type=jnp.float32
    )
    return (grad_query, grad_key, grad_value)


def assemble(slots, slot_live, owner_shard, keys_local, values_local):
    qblocks, topk = owner_shard.shape
    tokens = keys_local.shape[0]
    width = KEY_VALUE_HEADS * DH
    memory_len = topk * BLK
    picked = jnp.take(slots, owner_shard.reshape(-1), axis=0)
    mem_keys = picked[..., :width].reshape(qblocks, memory_len, KEY_VALUE_HEADS, DH)
    mem_values = picked[..., width:].reshape(qblocks, memory_len, KEY_VALUE_HEADS, DH)
    key_rows = jnp.concatenate(
        [mem_keys, jnp.broadcast_to(keys_local[None], (qblocks, tokens, KEY_VALUE_HEADS, DH))],
        axis=1,
    )
    value_rows = jnp.concatenate(
        [mem_values, jnp.broadcast_to(values_local[None], (qblocks, tokens, KEY_VALUE_HEADS, DH))],
        axis=1,
    )
    live_len = jnp.take(slot_live[:, 0], owner_shard.reshape(-1))
    live_mask = (jnp.arange(BLK)[None, :] < live_len[:, None]).reshape(qblocks, memory_len)
    row_pos = jnp.arange(qblocks)[:, None] * BLK + jnp.arange(BLK)[None, :]
    causal = jnp.arange(tokens)[None, None, :] <= row_pos[:, :, None]
    key_mask = jnp.concatenate(
        [jnp.broadcast_to(live_mask[:, None, :], (qblocks, BLK, memory_len)), causal], axis=-1
    )
    return (
        jnp.transpose(key_rows, (2, 0, 1, 3)),
        jnp.transpose(value_rows, (2, 0, 1, 3)),
        key_mask,
    )


def per_device(qkv_rows, grad_output, memory_rows, shard_fill, block_ids):
    shards = lax.axis_size("mem")
    groups = H // KEY_VALUE_HEADS
    width = KEY_VALUE_HEADS * DH
    rows_here = qkv_rows[0, 0]
    tokens = rows_here.shape[0]
    ids_here = block_ids[0, 0]
    qblocks, topk = ids_here.shape
    memory_len = topk * BLK
    held_blocks = memory_rows.shape[1]
    queries = rows_here[:, : H * DH].reshape(qblocks, BLK, KEY_VALUE_HEADS, groups, DH)
    keys_local = rows_here[:, H * DH : (H + KEY_VALUE_HEADS) * DH].reshape(
        tokens, KEY_VALUE_HEADS, DH
    )
    values_local = rows_here[:, (H + KEY_VALUE_HEADS) * DH :].reshape(tokens, KEY_VALUE_HEADS, DH)
    grad_rows = grad_output[0, 0].reshape(qblocks, BLK, KEY_VALUE_HEADS, groups, DH)
    queries_head = jnp.transpose(queries, (2, 0, 1, 3, 4))
    grads_head = jnp.transpose(grad_rows, (2, 0, 1, 3, 4))
    owner_shard = ids_here // held_blocks
    slot_index = ids_here % held_blocks
    shard_ids = jnp.arange(shards, dtype=jnp.int32)
    hits = owner_shard[:, :, None] == shard_ids[None, None, :]
    request = jnp.max(jnp.where(hits, slot_index[:, :, None], -1), axis=(0, 1))
    wanted = lax.all_to_all(request[:, None], "mem", split_axis=0, concat_axis=0, tiled=True)[:, 0]
    picked = jnp.take(memory_rows[0], jnp.maximum(wanted, 0), axis=0)
    live_len = jnp.where(wanted >= 0, jnp.clip(shard_fill[0, 0] - wanted * BLK, 0, BLK), 0)[:, None]
    slots, slot_live = (
        lax.all_to_all(picked, "mem", split_axis=0, concat_axis=0, tiled=True),
        lax.all_to_all(live_len, "mem", split_axis=0, concat_axis=0, tiled=True),
    )
    key_rows, value_rows, key_mask = assemble(
        slots, slot_live, owner_shard, keys_local, values_local
    )
    log_total, attended = lax.map(
        partial(head_forward, key_mask), (queries_head, key_rows, value_rows)
    )
    served_again = lax.optimization_barrier((picked, live_len, log_total))
    slots_back, live_back = (
        lax.all_to_all(served_again[0], "mem", split_axis=0, concat_axis=0, tiled=True),
        lax.all_to_all(served_again[1], "mem", split_axis=0, concat_axis=0, tiled=True),
    )
    key_rows, value_rows, key_mask = assemble(
        slots_back, live_back, owner_shard, keys_local, values_local
    )
    grad_query, grad_key, grad_value = lax.map(
        partial(head_backward, key_mask),
        (queries_head, key_rows, value_rows, grads_head, log_total, attended),
    )
    query_part = jnp.transpose(grad_query, (1, 2, 0, 3, 4)).reshape(tokens, H * DH)
    local_key = jnp.transpose(jnp.sum(grad_key[:, :, memory_len:], axis=1), (1, 0, 2)).reshape(
        tokens, width
    )
    local_value = jnp.transpose(jnp.sum(grad_value[:, :, memory_len:], axis=1), (1, 0, 2)).reshape(
        tokens, width
    )
    section_grads = jnp.concatenate([query_part, local_key, local_value], axis=-1).astype(
        jnp.bfloat16
    )
    upstream = passed_along(section_grads[None, None], "section", -1)
    mem_key_grad = jnp.transpose(grad_key[:, :, :memory_len], (1, 2, 0, 3)).reshape(
        qblocks, topk, BLK * width
    )
    mem_value_grad = jnp.transpose(grad_value[:, :, :memory_len], (1, 2, 0, 3)).reshape(
        qblocks, topk, BLK * width
    )
    key_slot = jnp.sum(jnp.where(hits, jnp.arange(topk, dtype=jnp.int32)[None, :, None], 0), axis=1)
    present = jnp.any(hits, axis=1)[:, :, None, None]
    entry_grads = jnp.concatenate(
        [
            mem_key_grad.reshape(qblocks, topk, BLK, width),
            mem_value_grad.reshape(qblocks, topk, BLK, width),
        ],
        axis=-1,
    )
    placed = jnp.take_along_axis(entry_grads, key_slot[:, :, None, None], axis=1)
    slot_grads = jnp.sum(jnp.where(present, placed, jnp.float32(0.0)), axis=0).astype(jnp.bfloat16)
    received = lax.all_to_all(slot_grads, "mem", split_axis=0, concat_axis=0, tiled=True)
    wanted_hot = (wanted[:, None] == jnp.arange(held_blocks, dtype=jnp.int32)[None, :]).astype(
        jnp.bfloat16
    )
    owned = jnp.einsum(
        "rj,rx->jx",
        wanted_hot,
        received.reshape(shards, BLK * 2 * width),
        preferred_element_type=jnp.float32,
    )
    summed = lax.psum(owned, "dp")
    memory_grad = summed.astype(jnp.bfloat16).reshape(1, held_blocks, BLK, 2 * width)
    return (upstream, memory_grad)


def solution(mesh):
    placed = (
        P("section", ("dp", "mem"), None, None),
        P("section", ("dp", "mem"), None, None),
        P("section", "mem", None, None),
        P("section", "mem"),
        P("section", ("dp", "mem"), None, None),
    )
    return jax.shard_map(
        per_device,
        mesh=mesh,
        in_specs=placed,
        out_specs=(P("section", ("dp", "mem"), None, None), P("section", "mem", None, None)),
        check_vma=False,
    )
```

profile of v0, /device:TPU:1, one launch (start us, length us, event | category | flops | bytes accessed | tf_op | source)
XLA Modules:
  0.0 475.6 jit_solution(16670266246849484863)
XLA Ops:
  2.2 10.5 %all-to-all-start = ((s32[32,1,1]{2,1,0:T(1,128)}), s32[32,1,1]{2,1,0:T(1,128)S(1)}, u32[]{:S(2)}, u32[]{:S(2)}) async-start(s32[32,1,1]{2,1,0:T(1,128)} %copy.52), calls=%async_computation | async-start | bytes 32768 | tf_op jit(solution)/shard_map/all_to_all | solution.py:117
  13.4 7.9 %all-to-all-done = s32[32,1,1]{2,1,0:T(1,128)S(1)} async-done(((s32[32,1,1]{2,1,0:T(1,128)}), s32[32,1,1]{2,1,0:T(1,128)S(1)}, u32[]{:S(2)}, u32[]{:S(2)}) %all-to-all-start) | async-done | bytes 160 | tf_op jit(solution)/shard_map/all_to_all | solution.py:117
  21.2 2.2 fusion.50
  23.5 3.8 all-to-all-start.1
  27.4 2.8 gather_fusion
  30.2 4.6 broadcast_select_fusion
  35.9 8.4 %all-to-all-start.2 = ((bf16[32,64,1024]{2,1,0:T(8,128)(2,1)}), bf16[32,64,1024]{2,1,0:T(8,128)(2,1)}, u32[]{:S(2)}, u32[]{:S(2)}) async-start(bf16[32,64,1024]{2,1,0:T(8,128)(2,1)} %broadcast_select_fusion), calls=%async_computation.2 | async-start | bytes 8388608 | tf_op jit(solution)/shard_map/all_to_all | solution.py:121
  49.0 87.9 %all-to-all-done.2 = bf16[32,64,1024]{2,1,0:T(8,128)(2,1)} async-done(((bf16[32,64,1024]{2,1,0:T(8,128)(2,1)}), bf16[32,64,1024]{2,1,0:T(8,128)(2,1)}, u32[]{:S(2)}, u32[]{:S(2)}) %all-to-all-start.2) | async-done | bytes 4194336 | tf_op jit(solution)/shard_map/all_to_all | solution.py:121
  136.9 2.9 gather_fusion.3
  145.2 15.3 %while.26 = (s32[]{:T(128)}, f32[4,2,64,4,1]{2,3,1,4,0:T(4,128)S(1)}, bf16[4,2,64,4,128]{4,2,3,1,0:T(8,128)(2,1)}, pred[2,64,640]{2,1,0:T(8,128)(4,1)S(1)}, bf16...) while((s32[]{:T(128)}, ...), condition=%wide.region_4.7_spmd, body=%wide.region_1.6_spmd.sunk | while | flops 170130944 | bytes 4958305 | solution.py:127
  145.2 1.4 fusion.76
  147.0 2.0 fusion.77
  149.0 1.4 fusion.76
  150.8 2.0 fusion.77
  152.9 1.4 fusion.76
  154.6 2.0 fusion.77
  156.7 1.4 fusion.76
  158.5 2.0 fusion.77
  160.6 14.7 %all_to_all.42 = s32[32,1,1]{2,1,0:T(1,128)S(1)} all-to-all(s32[32,1,1]{2,1,0:T(1,128)S(1)} %copy.56), channel_id=1, replica_groups=mesh['dp'=2,'section'=8,'mem'=32] {'mem'}, dimensions={0} | all-to-all | bytes 256 | tf_op jit(solution)/shard_map/all_to_all | solution.py:133
  175.3 5.2 %all-to-all-start.4 = ((bf16[32,64,1024]{2,1,0:T(8,128)(2,1)}), bf16[32,64,1024]{2,1,0:T(8,128)(2,1)}, u32[]{:S(2)}, u32[]{:S(2)}) async-start(bf16[32,64,1024]{2,1,0:T(8,128)(2,1)} %broadcast_select_fusion), calls=%async_computation.4 | async-start | bytes 8388608 | tf_op jit(solution)/shard_map/all_to_all | solution.py:132
  184.2 86.3 %all-to-all-done.4 = bf16[32,64,1024]{2,1,0:T(8,128)(2,1)} async-done(((bf16[32,64,1024]{2,1,0:T(8,128)(2,1)}), bf16[32,64,1024]{2,1,0:T(8,128)(2,1)}, u32[]{:S(2)}, u32[]{:S(2)}) %all-to-all-start.4) | async-done | bytes 4194336 | tf_op jit(solution)/shard_map/all_to_all | solution.py:132
  270.5 2.9 gather_fusion.5
  277.7 36.5 %while.27 = (s32[]{:T(128)}, bf16[4,2,64,4,128]{4,2,3,1,0:T(8,128)(2,1)}, f32[4,2,640,128]{3,2,1,0:T(8,128)}, f32[4,2,640,128]{3,2,1,0:T(8,128)}, pred[2,64,640]...) while((s32[]{:T(128)}, ...), condition=%wide.region_7.10_spmd, body=%wide.region_5.9_spmd.sunk | while | flops 422215168 | bytes 9600145 | solution.py:138
  279.8 1.4 fusion.86
  284.7 2.1 fusion.90
  288.8 1.4 fusion.86
  290.2 1.3 fusion.88
  293.7 2.2 fusion.90
  297.9 1.4 fusion.86
  302.9 2.2 fusion.90
  307.0 1.4 fusion.86
  308.4 1.3 fusion.88
  310.7 1.3 fusion.91
  312.0 2.2 fusion.90
  314.2 3.9 slice_bitcast_fusion
  318.1 1.4 copy.67
  319.4 1.9 reshape_reshape.7
  321.3 2.9 copy.66
  324.3 1.9 reshape_reshape.6
  326.1 4.7 pad_maximum_fusion
  330.8 11.5 %gather_fusion.1 = f32[64,64,1024]{2,1,0:T(8,128)} fusion(f32[2,8,64,1024]{3,2,1,0:T(8,128)} %pad_maximum_fusion, s32[64]{0:T(128)S(1)} %reshape.373), kind=kCustom, calls=%fused_computation.5 | custom fusion | bytes 33554944 | tf_op jit(solution)/shard_map/jit(take_along_axis)/gather | solution.py:168
  342.3 10.5 %select_reduce_fusion = bf16[32,64,1024]{2,1,0:T(8,128)(2,1)} fusion(f32[2,32,64,1024]{3,2,1,0:T(8,128)} %bitcast.186, pred[2,32]{1,0:T(4,128)(4,1)S(1)} %compare_and_fusion.1, pred[2,32]{1,0:T(4,128)(4,1)S(1)} %fusion.45), kind=kLoop, calls=%fused_computation.60 | loop fusion | flops 10485760 | bytes 20971648 | tf_op jit(solution)/shard_map/reduce_sum | solution.py:169
  352.8 7.6 %all-to-all-start.5 = ((bf16[32,64,1024]{2,1,0:T(8,128)(2,1)}), bf16[32,64,1024]{2,1,0:T(8,128)(2,1)}, u32[]{:S(2)}, u32[]{:S(2)}) async-start(bf16[32,64,1024]{2,1,0:T(8,128)(2,1)} %select_reduce_fusion), calls=%async_computation.5 | async-start | bytes 8388608 | tf_op jit(solution)/shard_map/all_to_all | solution.py:170
  364.5 16.3 %collective-permute-done = bf16[1,1,128,3072]{3,2,1,0:T(8,128)(2,1)S(1)} collective-permute-done((bf16[1,1,128,3072]{3,2,1,0:T(8,128)(2,1)S(1)}, bf16[1,1,128,3072]{3,2,1,0:T(8,128)(2,1)S(1)}, u32[]{:S(2)}, u32[]{:S(2)}) %collective-permute-start) | collective-permute-done | bytes 786464 | tf_op jit(solution)/shard_map/ppermute | solution.py:17
  380.8 69.6 %all-to-all-done.5 = bf16[32,64,1024]{2,1,0:T(8,128)(2,1)} async-done(((bf16[32,64,1024]{2,1,0:T(8,128)(2,1)}), bf16[32,64,1024]{2,1,0:T(8,128)(2,1)}, u32[]{:S(2)}, u32[]{:S(2)}) %all-to-all-start.5) | async-done | bytes 4194336 | tf_op jit(solution)/shard_map/all_to_all | solution.py:170
  450.4 4.5 copy.76
  455.7 16.2 %all-reduce.1 = bf16[8,65536]{1,0:T(8,128)(2,1)} all-reduce(f32[8,65536]{1,0:T(8,128)S(1)} %fusion.43), channel_id=1, replica_groups=mesh['dp'=2,'section'=8,'mem'=32] {'dp'}, use_global_device_ids=true, to_apply=%region_13.16 | all-reduce | flops 524288 | bytes 3145728 | tf_op jit(solution)/shard_map/psum | solution.py:180
  471.9 2.8 copy.68
  (131 shorter events, 46.4 us)
Async XLA Ops:
  0.6 26.7 %copy-start = (bf16[1,8,64,1024]{3,2,1,0:T(8,128)(2,1)S(1)}, bf16[1,8,64,1024]{3,2,1,0:T(8,128)(2,1)}, u32[]{:S(2)}) copy-start(bf16[1,8,64,1024]{3,2,1,0:T(8,128)(2,1)} %param.15) | copy-start | bytes 3145732
  2.2 19.0 %all-to-all-start = ((s32[32,1,1]{2,1,0:T(1,128)}), s32[32,1,1]{2,1,0:T(1,128)S(1)}, u32[]{:S(2)}, u32[]{:S(2)}) async-start(s32[32,1,1]{2,1,0:T(1,128)} %copy.52), calls=%async_computation | async-start | bytes 32768 | tf_op jit(solution)/shard_map/all_to_all | solution.py:117
  23.5 12.4 %all-to-all-start.1 = ((s32[32,1,1]{2,1,0:T(1,128)}), s32[32,1,1]{2,1,0:T(1,128)S(1)}, u32[]{:S(2)}, u32[]{:S(2)}) async-start(s32[32,1,1]{2,1,0:T(1,128)} %get-tuple-element.237), calls=%async_computation.1 | async-start | bytes 32768 | tf_op jit(solution)/shard_map/all_to_all | solution.py:122
  34.8 9.5 %copy-start.11 = (s32[1,1,2,8]{3,2,1,0:T(2,128)S(1)}, s32[1,1,2,8]{3,2,1,0:T(2,128)}, u32[]{:S(2)}) copy-start(s32[1,1,2,8]{3,2,1,0:T(2,128)} %param.17) | copy-start | bytes 196
  34.8 9.7 %copy-start.6 = (bf16[1,1,128,3072]{3,2,1,0:T(8,128)(2,1)S(1)}, bf16[1,1,128,3072]{3,2,1,0:T(8,128)(2,1)}, u32[]{:S(2)}) copy-start(bf16[1,1,128,3072]{3,2,1,0:T(8,128)(2,1)} %param.13) | copy-start | bytes 2359300
  35.9 101.0 %all-to-all-start.2 = ((bf16[32,64,1024]{2,1,0:T(8,128)(2,1)}), bf16[32,64,1024]{2,1,0:T(8,128)(2,1)}, u32[]{:S(2)}, u32[]{:S(2)}) async-start(bf16[32,64,1024]{2,1,0:T(8,128)(2,1)} %broadcast_select_fusion), calls=%async_computation.2 | async-start | bytes 8388608 | tf_op jit(solution)/shard_map/all_to_all | solution.py:121
  142.5 1.6 copy-start.7
  144.1 1.0 copy-start.2
  175.3 5.3 %copy-start.8 = (bf16[1,1,128,2048]{3,2,1,0:T(8,128)(2,1)S(1)}, bf16[1,1,128,2048]{3,2,1,0:T(8,128)(2,1)}, u32[]{:S(2)}) copy-start(bf16[1,1,128,2048]{3,2,1,0:T(8,128)(2,1)} %param.14) | copy-start | bytes 1572868
  175.3 95.2 %all-to-all-start.4 = ((bf16[32,64,1024]{2,1,0:T(8,128)(2,1)}), bf16[32,64,1024]{2,1,0:T(8,128)(2,1)}, u32[]{:S(2)}, u32[]{:S(2)}) async-start(bf16[32,64,1024]{2,1,0:T(8,128)(2,1)} %broadcast_select_fusion), calls=%async_computation.4 | async-start | bytes 8388608 | tf_op jit(solution)/shard_map/all_to_all | solution.py:132
  275.1 1.6 copy-start.3
  276.7 1.0 copy-start.10
  352.8 7.6 %copy-start.9 = (bf16[4,2,64,4,128]{4,2,3,1,0:T(8,128)(2,1)S(1)}, bf16[4,2,64,4,128]{4,2,3,1,0:T(8,128)(2,1)}, u32[]{:S(2)}) copy-start(bf16[4,2,64,4,128]{4,2,3,1,0:T(8,128)(2,1)} %get-tuple-element.107) | copy-start | bytes 1572868
  352.8 97.5 %all-to-all-start.5 = ((bf16[32,64,1024]{2,1,0:T(8,128)(2,1)}), bf16[32,64,1024]{2,1,0:T(8,128)(2,1)}, u32[]{:S(2)}, u32[]{:S(2)}) async-start(bf16[32,64,1024]{2,1,0:T(8,128)(2,1)} %select_reduce_fusion), calls=%async_computation.5 | async-start | bytes 8388608 | tf_op jit(solution)/shard_map/all_to_all | solution.py:170
  363.2 17.6 %collective-permute-start = (bf16[1,1,128,3072]{3,2,1,0:T(8,128)(2,1)S(1)}, bf16[1,1,128,3072]{3,2,1,0:T(8,128)(2,1)S(1)}, u32[]{:S(2)}, u32[]{:S(2)}) collective-permute-start(bf16[1,1,128,3072]{3,2,1,0:T(8,128)(2,1)S(1)} %pad_maximum_fusion.5), channel_id=1, source_target_pairs={{32,0},{64,32},{96,64},{128,96},{160,128},{192,160},{224,192},{33,... | collective-permute-start | bytes 2359304 | tf_op jit(solution)/shard_map/ppermute | solution.py:17
  380.8 74.1 %copy-start.4 = (bf16[1,1,128,3072]{3,2,1,0:T(8,128)(2,1)}, bf16[1,1,128,3072]{3,2,1,0:T(8,128)(2,1)S(1)}, u32[]{:S(2)}) copy-start(bf16[1,1,128,3072]{3,2,1,0:T(8,128)(2,1)S(1)} %collective-permute-done) | copy-start | bytes 2359300
  455.7 20.0 %copy-start.1 = (bf16[1,8,64,1024]{3,2,1,0:T(8,128)(2,1)S(1)}, bf16[1,8,64,1024]{3,2,1,0:T(8,128)(2,1)}, u32[]{:S(2)}) copy-start(bf16[1,8,64,1024]{3,2,1,0:T(8,128)(2,1)} %param.15) | copy-start | bytes 3145732
  471.9 2.9 copy-start.5
where the time goes:
time: 477 us; the launch traced here: 476 us
  waiting for transfers between devices  269 us (56%)
  local copies, waits for them, and re-layouts  57.8 us (12%)
  matrix products  42.7 us (9%)
  starting transfers between devices  36.8 us (8%)
  other arithmetic  36.4 us (8%)
  blocking collectives  31 us (6%)
    all_to_all x1, waiting for transfers between devices, per_device(): lax.all_to_all(picked, 'mem', split_axis=0, concat_axis=0, tiled=True)  87.9 us
    all_to_all x1, waiting for transfers between devices, per_device(): lax.all_to_all(served_again[0], 'mem', split_axis=0, concat_axis=0, tiled...  86.3 us
    all_to_all x1, waiting for transfers between devices, per_device(): lax.all_to_all(slot_grads, 'mem', split_axis=0, concat_axis=0, tiled=True)  69.6 us
    ppermute x1, waiting for transfers between devices, passed_along(): return lax.ppermute(array, axis, pairs)  16.3 us
    psum x1, blocking collectives, per_device(): summed = lax.psum(owned, 'dp')  16.2 us
    all_to_all x1, blocking collectives, per_device(): lax.all_to_all(served_again[1], 'mem', split_axis=0, concat_axis=0, tiled...  14.7 us
    gather x2, local copies, waits for them, and re-layouts, per_device(): jnp.take_along_axis(entry_grads, key_slot[:, :, None, None], axis=1)  11.6 us
    dot_general x8, matrix products, head_scores(): jnp.einsum('bihd,bnd->bihn', queries, key_rows, preferred_element_type=jn...  10.8 us
  transfers between devices with their start and end apart: 6, of which 6 were waited for; matrix products, arithmetic and copies ran while one was open for 4% of the time, Pallas kernels for 0%

commit v1 on v0

--- a/solution.py
+++ b/solution.py
@@ -177,7 +177,7 @@
         received.reshape(shards, BLK * 2 * width),
         preferred_element_type=jnp.float32,
     )
-    summed = lax.psum(owned, "dp")
+    summed = jnp.sum(lax.all_gather(owned, "dp"), axis=0)
     memory_grad = summed.astype(jnp.bfloat16).reshape(1, held_blocks, BLK, 2 * width)
     return (upstream, memory_grad)
 

time: 477 us -> 502 us (1.052)
  blocking collectives: 31 us -> 112 us
  waiting for transfers between devices: 269 us -> 208 us
  between operations: 1.76 us -> 15.1 us
  starting transfers between devices: 36.8 us -> 29 us
    all_to_all x0 -> x1, blocking collectives: none -> 97.4 us  [per_device(): lax.all_to_all(slot_grads, 'mem', split_axis=0, concat_axis=0, tiled=True)]
    all_to_all x1 -> x0, waiting for transfers between devices: 69.6 us -> none  [per_device(): lax.all_to_all(slot_grads, 'mem', split_axis=0, concat_axis=0, tiled=True)]
    psum x1 -> x0, blocking collectives: 16.2 us -> none  [per_device(): summed = lax.psum(owned, 'dp')]
    all_gather x0 -> x1, waiting for transfers between devices: none -> 9.78 us  [per_device(): summed = jnp.sum(lax.all_gather(owned, 'dp'), axis=0)]
    all_to_all x1 -> x0, starting transfers between devices: 7.62 us -> none  [per_device(): lax.all_to_all(slot_grads, 'mem', split_axis=0, concat_axis=0, tiled=True)]
where the time goes in v1:
time: 502 us; the launch traced here: 501 us
  waiting for transfers between devices  208 us (41%)
  blocking collectives  112 us (22%)
  local copies, waits for them, and re-layouts  55.3 us (11%)
  matrix products  44 us (9%)
  other arithmetic  37.4 us (7%)
  starting transfers between devices  29 us (6%)
  between operations  15.1 us (3%)
    all_to_all x1, blocking collectives, per_device(): lax.all_to_all(slot_grads, 'mem', split_axis=0, concat_axis=0, tiled=True)  97.4 us
    all_to_all x1, waiting for transfers between devices, per_device(): lax.all_to_all(picked, 'mem', split_axis=0, concat_axis=0, tiled=True)  87.9 us
    all_to_all x1, waiting for transfers between devices, per_device(): lax.all_to_all(served_again[0], 'mem', split_axis=0, concat_axis=0, tiled...  86.5 us
    all_to_all x1, blocking collectives, per_device(): lax.all_to_all(served_again[1], 'mem', split_axis=0, concat_axis=0, tiled...  14.7 us
    ppermute x1, waiting for transfers between devices, passed_along(): return lax.ppermute(array, axis, pairs)  14.4 us
    gather x2, local copies, waits for them, and re-layouts, per_device(): jnp.take_along_axis(entry_grads, key_slot[:, :, None, None], axis=1)  11.4 us
    dot_general x8, matrix products, head_scores(): jnp.einsum('bihd,bnd->bihn', queries, key_rows, preferred_element_type=jn...  10.8 us
    all_to_all x1, starting transfers between devices, per_device(): lax.all_to_all(request[:, None], 'mem', split_axis=0, concat_axis=0, tile...  10.5 us
  transfers between devices with their start and end apart: 6, of which 6 were waited for; matrix products, arithmetic and copies ran while one was open for 4% of the time, Pallas kernels for 0%

profile of v1, /device:TPU:1, one launch (start us, length us, event | category | flops | bytes accessed | tf_op | source)
XLA Modules:
  0.0 500.7 jit_solution(5172365711403133862)
XLA Ops:
  8.7 10.5 %all-to-all-start = ((s32[32,1,1]{2,1,0:T(1,128)}), s32[32,1,1]{2,1,0:T(1,128)S(1)}, u32[]{:S(2)}, u32[]{:S(2)}) async-start(s32[32,1,1]{2,1,0:T(1,128)} %copy.48), calls=%async_computation | async-start | bytes 32768 | tf_op jit(solution)/shard_map/all_to_all | solution.py:117
  19.9 7.9 %all-to-all-done = s32[32,1,1]{2,1,0:T(1,128)S(1)} async-done(((s32[32,1,1]{2,1,0:T(1,128)}), s32[32,1,1]{2,1,0:T(1,128)S(1)}, u32[]{:S(2)}, u32[]{:S(2)}) %all-to-all-start) | async-done | bytes 160 | tf_op jit(solution)/shard_map/all_to_all | solution.py:117
  27.8 2.2 fusion.50
  30.0 3.8 all-to-all-start.1
  33.9 2.8 gather_fusion
  36.7 4.6 broadcast_select_fusion
  42.4 8.4 %all-to-all-start.2 = ((bf16[32,64,1024]{2,1,0:T(8,128)(2,1)}), bf16[32,64,1024]{2,1,0:T(8,128)(2,1)}, u32[]{:S(2)}, u32[]{:S(2)}) async-start(bf16[32,64,1024]{2,1,0:T(8,128)(2,1)} %broadcast_select_fusion), calls=%async_computation.2 | async-start | bytes 8388608 | tf_op jit(solution)/shard_map/all_to_all | solution.py:121
  55.6 87.9 %all-to-all-done.2 = bf16[32,64,1024]{2,1,0:T(8,128)(2,1)} async-done(((bf16[32,64,1024]{2,1,0:T(8,128)(2,1)}), bf16[32,64,1024]{2,1,0:T(8,128)(2,1)}, u32[]{:S(2)}, u32[]{:S(2)}) %all-to-all-start.2) | async-done | bytes 4194336 | tf_op jit(solution)/shard_map/all_to_all | solution.py:121
  143.5 2.9 gather_fusion.3
  151.7 15.3 %while.26 = (s32[]{:T(128)}, f32[4,2,64,4,1]{2,3,1,4,0:T(4,128)S(1)}, bf16[4,2,64,4,128]{4,2,3,1,0:T(8,128)(2,1)}, pred[2,64,640]{2,1,0:T(8,128)(4,1)S(1)}, bf16...) while((s32[]{:T(128)}, ...), condition=%wide.region_4.7_spmd, body=%wide.region_1.6_spmd.sunk | while | flops 170130944 | bytes 4958305 | solution.py:127
  151.7 1.4 fusion.76
  153.5 2.0 fusion.77
  155.6 1.4 fusion.76
  157.3 2.0 fusion.77
  159.4 1.4 fusion.76
  161.2 2.0 fusion.77
  163.2 1.4 fusion.76
  165.0 2.0 fusion.77
  167.1 14.7 %all_to_all.42 = s32[32,1,1]{2,1,0:T(1,128)S(1)} all-to-all(s32[32,1,1]{2,1,0:T(1,128)S(1)} %copy.52), channel_id=1, replica_groups=mesh['dp'=2,'section'=8,'mem'=32] {'mem'}, dimensions={0} | all-to-all | bytes 256 | tf_op jit(solution)/shard_map/all_to_all | solution.py:133
  181.9 5.0 all-to-all-start.4
  190.6 86.5 %all-to-all-done.4 = bf16[32,64,1024]{2,1,0:T(8,128)(2,1)} async-done(((bf16[32,64,1024]{2,1,0:T(8,128)(2,1)}), bf16[32,64,1024]{2,1,0:T(8,128)(2,1)}, u32[]{:S(2)}, u32[]{:S(2)}) %all-to-all-start.4) | async-done | bytes 4194336 | tf_op jit(solution)/shard_map/all_to_all | solution.py:132
  277.1 2.9 gather_fusion.5
  284.5 36.5 %while.27 = (s32[]{:T(128)}, bf16[4,2,64,4,128]{4,2,3,1,0:T(8,128)(2,1)}, f32[4,2,640,128]{3,2,1,0:T(8,128)}, f32[4,2,640,128]{3,2,1,0:T(8,128)}, pred[2,64,640]...) while((s32[]{:T(128)}, ...), condition=%wide.region_7.10_spmd, body=%wide.region_5.9_spmd.sunk | while | flops 422215168 | bytes 9600145 | solution.py:138
  286.5 1.4 fusion.86
  291.4 2.1 fusion.90
  295.6 1.4 fusion.86
  297.0 1.3 fusion.88
  300.5 2.2 fusion.90
  304.7 1.4 fusion.86
  309.6 2.2 fusion.90
  313.8 1.4 fusion.86
  315.2 1.3 fusion.88
  318.8 2.2 fusion.90
  321.0 3.9 slice_bitcast_fusion
  324.8 1.4 copy.63
  326.2 1.9 reshape_reshape.7
  328.1 2.9 copy.62
  331.0 1.9 reshape_reshape.6
  332.9 4.7 pad_maximum_fusion
  337.6 11.3 %gather_fusion.1 = f32[64,64,1024]{2,1,0:T(8,128)} fusion(f32[2,8,64,1024]{3,2,1,0:T(8,128)} %pad_maximum_fusion, s32[64]{0:T(128)S(1)} %reshape.381), kind=kCustom, calls=%fused_computation.5 | custom fusion | bytes 33554944 | tf_op jit(solution)/shard_map/jit(take_along_axis)/gather | solution.py:168
  348.9 8.8 %select_reduce_fusion = bf16[32,64,1024]{2,1,0:T(8,128)(2,1)S(1)} fusion(f32[2,32,64,1024]{3,2,1,0:T(8,128)} %bitcast.192, pred[2,32]{1,0:T(4,128)(4,1)S(1)} %compare_and_fusion.1, pred[2,32]{1,0:T(4,128)(4,1)S(1)} %fusion.45), kind=kLoop, calls=%fused_computation.60 | loop fusion | flops 10485760 | bytes 20971648 | tf_op jit(solution)/shard_map/reduce_sum | solution.py:169
  357.7 97.4 %all_to_all.43 = bf16[32,64,1024]{2,1,0:T(8,128)(2,1)S(1)} all-to-all(bf16[32,64,1024]{2,1,0:T(8,128)(2,1)S(1)} %select_reduce_fusion), channel_id=1, replica_groups=mesh['dp'=2,'section'=8,'mem'=32] {'mem'}, dimensions={0} | all-to-all | bytes 8388608 | tf_op jit(solution)/shard_map/all_to_all | solution.py:170
  455.1 2.4 copy.71
  457.4 2.1 fusion.43
  464.6 14.4 %collective-permute-done = bf16[1,1,128,3072]{3,2,1,0:T(8,128)(2,1)S(1)} collective-permute-done((bf16[1,1,128,3072]{3,2,1,0:T(8,128)(2,1)S(1)}, bf16[1,1,128,3072]{3,2,1,0:T(8,128)(2,1)S(1)}, u32[]{:S(2)}, u32[]{:S(2)}) %collective-permute-start) | collective-permute-done | bytes 786464 | tf_op jit(solution)/shard_map/ppermute | solution.py:17
  479.0 9.8 %all-gather.3.cloned.1.call-done = f32[16,65536]{1,0:T(8,128)} async-done(((f32[8,65536]{1,0:T(8,128)}), f32[16,65536]{1,0:T(8,128)}) %all-gather.3.cloned.1.call-update) | async-done | bytes 4194320 | tf_op jit(solution)/shard_map/all_gather | solution.py:180
  488.8 2.7 bitcast_reduce_fusion
  491.5 1.5 copy.79
  (129 shorter events, 48.1 us)
Async XLA Ops:
  7.2 26.7 %copy-start = (bf16[1,8,64,1024]{3,2,1,0:T(8,128)(2,1)S(1)}, bf16[1,8,64,1024]{3,2,1,0:T(8,128)(2,1)}, u32[]{:S(2)}) copy-start(bf16[1,8,64,1024]{3,2,1,0:T(8,128)(2,1)} %param.15) | copy-start | bytes 3145732
  8.7 19.0 %all-to-all-start = ((s32[32,1,1]{2,1,0:T(1,128)}), s32[32,1,1]{2,1,0:T(1,128)S(1)}, u32[]{:S(2)}, u32[]{:S(2)}) async-start(s32[32,1,1]{2,1,0:T(1,128)} %copy.48), calls=%async_computation | async-start | bytes 32768 | tf_op jit(solution)/shard_map/all_to_all | solution.py:117
  30.0 12.4 %all-to-all-start.1 = ((s32[32,1,1]{2,1,0:T(1,128)}), s32[32,1,1]{2,1,0:T(1,128)S(1)}, u32[]{:S(2)}, u32[]{:S(2)}) async-start(s32[32,1,1]{2,1,0:T(1,128)} %get-tuple-element.227), calls=%async_computation.1 | async-start | bytes 32768 | tf_op jit(solution)/shard_map/all_to_all | solution.py:122
  41.3 9.5 %copy-start.9 = (s32[1,1,2,8]{3,2,1,0:T(2,128)S(1)}, s32[1,1,2,8]{3,2,1,0:T(2,128)}, u32[]{:S(2)}) copy-start(s32[1,1,2,8]{3,2,1,0:T(2,128)} %param.17) | copy-start | bytes 196
  41.3 9.7 %copy-start.4 = (bf16[1,1,128,3072]{3,2,1,0:T(8,128)(2,1)S(1)}, bf16[1,1,128,3072]{3,2,1,0:T(8,128)(2,1)}, u32[]{:S(2)}) copy-start(bf16[1,1,128,3072]{3,2,1,0:T(8,128)(2,1)} %param.13) | copy-start | bytes 2359300
  42.4 101.0 %all-to-all-start.2 = ((bf16[32,64,1024]{2,1,0:T(8,128)(2,1)}), bf16[32,64,1024]{2,1,0:T(8,128)(2,1)}, u32[]{:S(2)}, u32[]{:S(2)}) async-start(bf16[32,64,1024]{2,1,0:T(8,128)(2,1)} %broadcast_select_fusion), calls=%async_computation.2 | async-start | bytes 8388608 | tf_op jit(solution)/shard_map/all_to_all | solution.py:121
  149.0 1.6 copy-start.5
  150.7 1.0 copy-start.2
  181.9 5.2 %copy-start.6 = (bf16[1,1,128,2048]{3,2,1,0:T(8,128)(2,1)S(1)}, bf16[1,1,128,2048]{3,2,1,0:T(8,128)(2,1)}, u32[]{:S(2)}) copy-start(bf16[1,1,128,2048]{3,2,1,0:T(8,128)(2,1)} %param.14) | copy-start | bytes 1572868
  181.9 95.2 %all-to-all-start.4 = ((bf16[32,64,1024]{2,1,0:T(8,128)(2,1)}), bf16[32,64,1024]{2,1,0:T(8,128)(2,1)}, u32[]{:S(2)}, u32[]{:S(2)}) async-start(bf16[32,64,1024]{2,1,0:T(8,128)(2,1)} %broadcast_select_fusion), calls=%async_computation.4 | async-start | bytes 8388608 | tf_op jit(solution)/shard_map/all_to_all | solution.py:132
  186.9 301.9 %all-gather.3.cloned.1.call-start = ((), (), s32[]{:S(2)}) async-start(), calls=%async_computation.6 | async-start | bytes 6291456 | tf_op jit(solution)/shard_map/all_gather | solution.py:180
  281.9 1.6 copy-start.3
  283.4 1.0 copy-start.8
  459.6 1.0 copy-start.7
  463.3 15.7 %collective-permute-start = (bf16[1,1,128,3072]{3,2,1,0:T(8,128)(2,1)S(1)}, bf16[1,1,128,3072]{3,2,1,0:T(8,128)(2,1)S(1)}, u32[]{:S(2)}, u32[]{:S(2)}) collective-permute-start(bf16[1,1,128,3072]{3,2,1,0:T(8,128)(2,1)S(1)} %pad_maximum_fusion.5), channel_id=1, source_target_pairs={{32,0},{64,32},{96,64},{128,96},{160,128},{192,160},{224,192},{33,... | collective-permute-start | bytes 2359304 | tf_op jit(solution)/shard_map/ppermute | solution.py:17
  488.8 5.1 %copy-start.1 = (bf16[1,8,64,1024]{3,2,1,0:T(8,128)(2,1)S(1)}, bf16[1,8,64,1024]{3,2,1,0:T(8,128)(2,1)}, u32[]{:S(2)}) copy-start(bf16[1,8,64,1024]{3,2,1,0:T(8,128)(2,1)} %param.15) | copy-start | bytes 3145732
Sparse Core Ops, SparseCore 0:
  459.7 28.9 all-gather.2
